TPU v7x, 256 devices: a whole 4x4x8 slice. The times are simulated.
256 devices in a mesh: cfg: 2 (over z_lo), req: 16 (over y, z_hi), mlp: 8 (over x, core).
Axes of the slice: x: 4, y: 4, z: 8 (z_hi: 4, z_lo: 2; z = z_hi * 2 + z_lo), core: 2. Of those that a mesh axis runs over, the one named last changes fastest.
Arguments:
- hidden: bfloat16 [2, 16384, 1152], P('cfg', ('req', 'mlp')), may hold values from -64 to 64
- noisy_latent: float32 [16384, 16], P(('req', 'mlp'), 'cfg'), may hold values from -6 to 6
- labels: int32 [16, 4], replicated, may hold values from 0 to 999
- timesteps: int32 [16, 4], replicated, may hold values from 0 to 999
- lengths: int32 [16, 4], P('req'), may hold values from 1 to 512, 1024 in all within a row
- guidance: float32 [16, 4], P('req'), may hold values from 1.5 to 4
- keep_scale: float32 [16, 4], P('req'), may hold values from 0.9 to 1.2
- noise_scale: float32 [16, 4], P('req'), may hold values from -0.8 to -0.2
- class_table: bfloat16 [1001, 1152], replicated, may hold values from -6 to 6
- time_up: bfloat16 [256, 1152], replicated, may hold values from -0.375 to 0.375
- time_up_bias: bfloat16 [1152], replicated, may hold values from -4 to 4
- time_out: bfloat16 [1152, 1152], replicated, may hold values from -0.1875 to 0.1875
- time_out_bias: bfloat16 [1152], replicated, may hold values from -4 to 4
- mod_weight: bfloat16 [1152, 9216], P(None, 'req'), may hold values from -0.1875 to 0.1875
- mod_bias: bfloat16 [9216], P('req'), may hold values from -4 to 4
- qkv_weight: bfloat16 [1152, 3456], P(None, 'req'), may hold values from -8 to 8
- qkv_bias: bfloat16 [3456], P('req'), may hold values from -4 to 4
- out_weight: bfloat16 [1152, 1152], P(None, 'req'), may hold values from -0.1875 to 0.1875
- out_bias: bfloat16 [1152], P('req'), may hold values from -4 to 4
- up_weight: bfloat16 [1152, 4608], P(None, 'mlp'), may hold values from -0.1875 to 0.1875
- up_bias: bfloat16 [4608], P('mlp'), may hold values from -4 to 4
- down_weight: bfloat16 [4608, 1152], P('mlp'), may hold values from -1 to 1
- down_bias: bfloat16 [1152], replicated, may hold values from -4 to 4
- final_weight: bfloat16 [1152, 16], replicated, may hold values from -0.1875 to 0.1875
- final_bias: bfloat16 [16], replicated, may hold values from -4 to 4
Outputs:
- next_latent: float32 [16384, 16], P(('req', 'mlp'), 'cfg')
Inputs may be any that keep to these rules, and one draw needn't show every extreme that they name: `lengths`: each row sums to 1024, and its largest crop has exactly 512 tokens.
All inputs are finite; a program needn't handle non-finite values.
Results may differ from a plain program's by a relative error of at most 0.015.
Values may be sent and summed in bfloat16 or wider, within the bound.
No kernel may reach another device: no remote copies, remote signals or barrier semaphores. Data moves between devices by JAX's collectives and lax.ppermute only.
A program may use at most 128 MiB of HBM per device.

v0:
```python
import math
import jax
import jax.numpy as jnp
from jax import lax
from jax.sharding import PartitionSpec as P

HEADS = 16
HEAD_DIM = 72
CLASSES = 1000
FREQ = 256


def layer_norm(values):
    values = values.astype(jnp.float32)
    centre = values - jnp.mean(values, axis=-1, keepdims=True)
    variance = jnp.mean(centre * centre, axis=-1, keepdims=True)
    return centre * lax.rsqrt(variance + 1e-06)


def time_features(times_flat):
    half_freq = FREQ // 2
    frequency = jnp.exp(-math.log(10000.0) * jnp.arange(half_freq, dtype=jnp.float32) / half_freq)
    angles = times_flat.astype(jnp.float32)[:, None] * frequency[None, :]
    return jnp.concatenate([jnp.cos(angles), jnp.sin(angles)], axis=1).astype(jnp.bfloat16)


def segment_ids(lengths_row, positions):
    ends = jnp.cumsum(lengths_row)
    return jnp.sum((positions[:, None] >= ends[None, :]).astype(jnp.int32), axis=1)


def attention(queries, keys_all, values_all, query_segment, key_segment):
    scores = jnp.einsum(
        "qhd,khd->hqk", queries, keys_all, preferred_element_type=jnp.float32
    ) / math.sqrt(HEAD_DIM)
    same = (query_segment[:, None] == key_segment[None, :])[None]
    masked = jnp.where(same, scores, -1e30)
    row_max = jnp.max(masked, axis=2, keepdims=True)
    expo = jnp.where(same, jnp.exp(masked - row_max), 0.0)
    denominator = jnp.sum(expo, axis=2)
    weights = expo.astype(jnp.bfloat16)
    mixed = jnp.einsum("hqk,khd->qhd", weights, values_all, preferred_element_type=jnp.float32)
    result = mixed / jnp.transpose(denominator)[:, :, None]
    return result.astype(jnp.bfloat16).reshape(queries.shape[0], -1)


def shards(
    hidden,
    noisy_latent,
    labels,
    timesteps,
    lengths,
    guidance,
    keep_scale,
    noise_scale,
    class_table,
    time_up,
    time_up_bias,
    time_out,
    time_out_bias,
    mod_weight,
    mod_bias,
    qkv_weight,
    qkv_bias,
    out_weight,
    out_bias,
    up_weight,
    up_bias,
    down_weight,
    down_bias,
    final_weight,
    final_bias,
):
    req_count = lax.axis_size("req")
    mlp_count = lax.axis_size("mlp")
    half_index = lax.axis_index("cfg")
    mlp_index = lax.axis_index("mlp")
    tok_rows = hidden.shape[1]
    width = hidden.shape[2]
    group_rows = tok_rows * mlp_count
    per_group = labels.shape[1]
    time_feat = time_features(timesteps.reshape(-1))
    time_mid = jax.nn.silu(
        jnp.dot(time_feat, time_up, preferred_element_type=jnp.float32)
        + time_up_bias.astype(jnp.float32)
    ).astype(jnp.bfloat16)
    time_cond = jnp.dot(
        time_mid, time_out, preferred_element_type=jnp.float32
    ) + time_out_bias.astype(jnp.float32)
    used_labels = jnp.where(half_index == 0, labels.reshape(-1), CLASSES)
    one_hot = (used_labels[:, None] == jnp.arange(CLASSES + 1, dtype=jnp.int32)[None, :]).astype(
        jnp.bfloat16
    )
    cond_act = jax.nn.silu(
        time_cond + jnp.dot(one_hot, class_table, preferred_element_type=jnp.float32)
    ).astype(jnp.bfloat16)
    local_mod = (
        jnp.dot(cond_act, mod_weight, preferred_element_type=jnp.float32)
        + mod_bias.astype(jnp.float32)
    ).astype(jnp.bfloat16)
    local_mod = local_mod.reshape(req_count, per_group, local_mod.shape[1])
    modulation = lax.all_to_all(local_mod, "req", split_axis=0, concat_axis=2, tiled=True)[0]
    positions = jnp.arange(group_rows, dtype=jnp.int32)
    segment_all = segment_ids(lengths[0], positions)
    segment_own = lax.dynamic_slice_in_dim(segment_all, mlp_index * tok_rows, tok_rows)
    member = segment_own[:, None] == jnp.arange(per_group, dtype=jnp.int32)[None, :]
    per_token = jnp.dot(member.astype(jnp.bfloat16), modulation, preferred_element_type=jnp.float32)
    pieces = [per_token[:, index * width : (index + 1) * width] for index in range(8)]
    shift_attn, scale_attn, gate_attn, shift_mlp, scale_mlp, gate_mlp, shift_final, scale_final = (
        pieces
    )
    rows = hidden[0]
    normed = (layer_norm(rows) * (1.0 + scale_attn) + shift_attn).astype(jnp.bfloat16)
    qkv_full, qkv_bias_full, out_full, out_bias_full = (
        lax.all_gather(qkv_weight, "req", axis=1, tiled=True),
        lax.all_gather(qkv_bias, "req", axis=0, tiled=True),
        lax.all_gather(out_weight, "req", axis=1, tiled=True),
        lax.all_gather(out_bias, "req", axis=0, tiled=True),
    )
    qkv = (
        jnp.dot(normed, qkv_full, preferred_element_type=jnp.float32)
        + qkv_bias_full.astype(jnp.float32)
    ).astype(jnp.bfloat16)
    keys_all, values_all = (
        lax.all_gather(qkv[:, width : 2 * width], "mlp", axis=0, tiled=True),
        lax.all_gather(qkv[:, 2 * width :], "mlp", axis=0, tiled=True),
    )
    attended = attention(
        qkv[:, :width].reshape(tok_rows, HEADS, HEAD_DIM),
        keys_all.reshape(group_rows, HEADS, HEAD_DIM),
        values_all.reshape(group_rows, HEADS, HEAD_DIM),
        segment_own,
        segment_all,
    )
    projected = jnp.dot(
        attended, out_full, preferred_element_type=jnp.float32
    ) + out_bias_full.astype(jnp.float32)
    mid_hidden = (rows.astype(jnp.float32) + gate_attn * projected).astype(jnp.bfloat16)
    normed_mlp = (layer_norm(mid_hidden) * (1.0 + scale_mlp) + shift_mlp).astype(jnp.bfloat16)
    gathered = lax.all_gather(normed_mlp, "mlp", axis=0, tiled=True)
    inner = jax.nn.gelu(
        jnp.dot(gathered, up_weight, preferred_element_type=jnp.float32)
        + up_bias.astype(jnp.float32),
        approximate=True,
    ).astype(jnp.bfloat16)
    mlp_out = lax.psum_scatter(
        jnp.dot(inner, down_weight, preferred_element_type=jnp.float32).astype(jnp.bfloat16),
        "mlp",
        scatter_dimension=0,
        tiled=True,
    ).astype(jnp.float32)
    final_hidden = mid_hidden.astype(jnp.float32) + gate_mlp * (
        mlp_out + down_bias.astype(jnp.float32)
    )
    normed_final = (layer_norm(final_hidden) * (1.0 + scale_final) + shift_final).astype(
        jnp.bfloat16
    )
    predicted = jnp.dot(
        normed_final, final_weight, preferred_element_type=jnp.float32
    ) + final_bias.astype(jnp.float32)
    halves = lax.all_to_all(predicted[None], "cfg", split_axis=2, concat_axis=0, tiled=True)
    eps_cond = halves[0]
    eps_free = halves[1]
    member_f = member.astype(jnp.float32)
    guide_tok = jnp.sum(member_f * guidance, axis=1, keepdims=True)
    keep_tok = jnp.sum(member_f * keep_scale, axis=1, keepdims=True)
    noise_tok = jnp.sum(member_f * noise_scale, axis=1, keepdims=True)
    return keep_tok * noisy_latent + noise_tok * (eps_free + guide_tok * (eps_cond - eps_free))


def solution(mesh):
    return jax.shard_map(
        shards,
        mesh=mesh,
        in_specs=(
            P("cfg", ("req", "mlp"), None),
            P(("req", "mlp"), "cfg"),
            P(),
            P(),
            P("req", None),
            P("req", None),
            P("req", None),
            P("req", None),
            P(),
            P(),
            P(),
            P(),
            P(),
            P(None, "req"),
            P("req"),
            P(None, "req"),
            P("req"),
            P(None, "req"),
            P("req"),
            P(None, "mlp"),
            P("mlp"),
            P("mlp", None),
            P(),
            P(),
            P(),
        ),
        out_specs=P(("req", "mlp"), "cfg"),
        check_vma=False,
    )
```

profile of v0, /device:TPU:8, one launch (start us, length us, event | category | flops | bytes accessed | tf_op | source)
XLA Modules:
  0.0 357.1 jit_solution(16776291229437060213)
XLA Ops:
  11.4 1.8 convolution_add_fusion.3
  13.2 3.0 fusion.29
  16.9 11.6 %all-to-all-start = ((bf16[16,4,576]{2,1,0:T(4,128)(2,1)}), bf16[16,4,576]{2,1,0:T(4,128)(2,1)S(1)}, u32[]{:S(2)}, u32[]{:S(2)}) async-start(bf16[16,4,576]{2,1,0:T(4,128)(2,1)} %reshape.143), calls=%async_computation | async-start | bytes 163840 | tf_op jit(solution)/shard_map/all_to_all | solution.py:102
  31.1 82.8 %all-reduce.2 = (bf16[3456]{0:T(1024)(128)(2,1)S(1)}, bf16[1152]{0:T(1024)(128)(2,1)S(1)}) all-reduce(bf16[3456]{0:T(1024)(128)(2,1)S(1)} %dynamic-update-slice, bf16[1152]{0:T(1024)(128)(2,1)S(1)} %dynamic-update-slice.1), channel_id=1, replica_groups=mesh['cfg'=2,'req'=16,'mlp'=8] {'req'}, use_global_device_ids=true, to_apply=%add | all-reduce | flops 4608 | bytes 18432
  114.6 3.0 fusion.67
  117.6 6.1 %fusion.2 = bf16[128,3456]{1,0:T(8,128)(2,1)S(1)} fusion(bf16[1152,3456]{0,1:T(8,128)(2,1)} %all-gather.6.cloned.1.call-done, f32[3456]{0:T(1024)S(1)} %convert_element_type.103, bf16[1,128,1152]{2,1,0:T(8,128)(2,1)S(1)} %copy-done.1, f32[128,9216]{1,0:T(8,128)} %fusion.67, f32[128]{0:T(128)S(1)} %add_rsqrt_fusion.2, f32[128]{0:T(128)S(1)} %broadcast_multiply_fusion.2), kind=kOutput, calls=%fused_computation.5 | convolution fusion | flops 1021132800 | bytes 10336768 | tf_op jit(solution)/shard_map/dot_general | solution.py:121
  123.7 0.9 fusion.83
  126.2 0.8 broadcast_compare_fusion
  127.2 37.7 %all-gather.10.cloned.1.call-done = bf16[1024,1152]{1,0:T(8,128)(2,1)} async-done(((bf16[128,1152]{1,0:T(8,128)(2,1)}), bf16[1024,1152]{1,0:T(8,128)(2,1)}) %all-gather.10.cloned.1.call-update) | async-done | bytes 2359312 | tf_op jit(solution)/shard_map/all_gather | solution.py:125
  164.9 4.3 %copy.52 = bf16[1024,1152]{0,1:T(8,128)(2,1)} copy(bf16[1024,1152]{1,0:T(8,128)(2,1)} %all-gather.10.cloned.1.call-done) | data formatting | bytes 4718592 | tf_op jit(solution)/shard_map/all_gather | solution.py:125
  169.2 26.3 %all-gather.8.cloned.1.call-done = bf16[1024,1152]{1,0:T(8,128)(2,1)} async-done(((bf16[128,1152]{1,0:T(8,128)(2,1)}), bf16[1024,1152]{1,0:T(8,128)(2,1)}) %all-gather.8.cloned.1.call-update) | async-done | bytes 2359312 | tf_op jit(solution)/shard_map/all_gather | solution.py:126
  195.5 4.3 %copy.50 = bf16[1024,1152]{0,1:T(8,128)(2,1)} copy(bf16[1024,1152]{1,0:T(8,128)(2,1)} %all-gather.8.cloned.1.call-done) | data formatting | bytes 4718592 | tf_op jit(solution)/shard_map/all_gather | solution.py:126
  199.8 7.5 %fusion.84 = (f32[16,128]{1,0:T(8,128)S(1)}, bf16[16,128,1024]{2,1,0:T(8,128)(2,1)}) fusion(pred[128,1024]{1,0:T(8,128)(4,1)S(1)} %copy-done.2, bf16[128,16,72]{0,2,1:T(8,128)(2,1)S(1)} %bitcast.88, bf16[1024,16,72]{0,2,1:T(8,128)(2,1)} %bitcast.84), kind=kOutput, calls=%fused_computation.112 | convolution fusion | flops 314573824 | bytes 6987776 | tf_op jit(solution)/shard_map/sub | solution.py:39
  207.2 5.2 %fusion.26 = bf16[128,16,72]{0,2,1:T(8,128)(2,1)} fusion(bf16[1024,16,72]{0,2,1:T(8,128)(2,1)} %bitcast.85, bf16[16,128,1024]{2,1,0:T(8,128)(2,1)} %get-tuple-element.18, f32[128,16]{0,1:T(8,128)S(1)} %bitcast.95), kind=kOutput, calls=%fused_computation.31 | convolution fusion | flops 302284800 | bytes 6856704 | tf_op jit(solution)/shard_map/hqk,khd->qhd/dot_general | solution.py:42
  212.4 49.4 %all-gather.12.cloned.1.call-done = bf16[1152,1152]{0,1:T(8,128)(2,1)} async-done(((bf16[1152,72]{0,1:T(8,128)(2,1)}), bf16[1152,1152]{0,1:T(8,128)(2,1)}) %all-gather.12.cloned.1.call-update) | async-done | bytes 2654224 | tf_op jit(solution)/shard_map/all_gather | solution.py:117
  261.8 3.0 fusion.85
  265.0 2.2 fusion.41
  267.3 26.1 %all-gather.14.cloned.1.call-done = bf16[1024,1152]{1,0:T(8,128)(2,1)} async-done(((bf16[128,1152]{1,0:T(8,128)(2,1)}), bf16[1024,1152]{1,0:T(8,128)(2,1)}) %all-gather.14.cloned.1.call-update) | async-done | bytes 2359312 | tf_op jit(solution)/shard_map/all_gather | solution.py:140
  293.4 7.8 %convolution_convert_fusion = bf16[1024,1152]{1,0:T(8,128)(2,1)} fusion(bf16[576,1152]{1,0:T(8,128)(2,1)} %param.46, bf16[1024,1152]{1,0:T(8,128)(2,1)} %all-gather.14.cloned.1.call-done, bf16[1152,576]{0,1:T(8,128)(2,1)} %param.44, f32[576]{0:T(1024)S(1)} %convert_element_type.111), kind=kOutput, calls=%fused_computation.11 | convolution fusion | flops 2724986880 | bytes 7375104 | tf_op jit(solution)/shard_map/dot_general | solution.py:147
  301.9 36.9 %reduce-scatter.2.cloned.1.call-done = bf16[128,1152]{1,0:T(8,128)(2,1)} async-done(((bf16[1024,1152]{1,0:T(8,128)(2,1)}), bf16[128,1152]{1,0:T(8,128)(2,1)}) %reduce-scatter.2.cloned.1.call-update) | async-done | bytes 294928 | tf_op jit(solution)/shard_map/reduce_scatter | solution.py:146
  338.8 1.3 fusion.81
  340.4 2.2 convolution_add_fusion.6
  342.6 3.2 all-to-all-start.1
  345.9 3.7 %all-to-all-done.1 = f32[1,128,16]{1,0,2:T(1,128)S(1)} async-done(((f32[1,128,16]{1,0,2:T(1,128)}), f32[1,128,16]{1,0,2:T(1,128)S(1)}, u32[]{:S(2)}, u32[]{:S(2)}) %all-to-all-start.1) | async-done | bytes 8224 | tf_op jit(solution)/shard_map/all_to_all | solution.py:161
  (84 shorter events, 11.1 us)
Async XLA Ops:
  6.5 4.8 %copy-start = (bf16[1152,1152]{1,0:T(8,128)(2,1)S(1)}, bf16[1152,1152]{1,0:T(8,128)(2,1)}, u32[]{:S(2)}) copy-start(bf16[1152,1152]{1,0:T(8,128)(2,1)} %param.36) | copy-start | bytes 7962628
  6.5 111.0 %all-gather.6.cloned.1.call-start = ((), (), s32[]{:S(2)}) async-start(), calls=%async_computation.3 | async-start | bytes 8460288 | tf_op jit(solution)/shard_map/all_gather | solution.py:115
  13.2 15.4 %copy-start.10 = (s32[1,4]{1,0:T(1,128)S(1)}, s32[1,4]{1,0:T(1,128)}, u32[]{:S(2)}) copy-start(s32[1,4]{1,0:T(1,128)} %param.29) | copy-start | bytes 52
  13.2 15.5 %copy-start.14 = (u32[256]{0:T(256)S(1)}, u32[256]{0:T(256)}, u32[]{:S(2)}) copy-start(u32[256]{0:T(256)} %constant.70) | copy-start | bytes 3076
  13.2 17.4 %copy-start.11 = (bf16[216]{0:T(256)(128)(2,1)S(1)}, bf16[216]{0:T(256)(128)(2,1)}, u32[]{:S(2)}) copy-start(bf16[216]{0:T(256)(128)(2,1)} %param.41) | copy-start | bytes 1300
  13.2 17.7 %copy-start.12 = (bf16[72]{0:T(256)(128)(2,1)S(1)}, bf16[72]{0:T(256)(128)(2,1)}, u32[]{:S(2)}) copy-start(bf16[72]{0:T(256)(128)(2,1)} %param.43) | copy-start | bytes 436
  13.2 100.9 %copy-start.1 = (bf16[1,128,1152]{2,1,0:T(8,128)(2,1)S(1)}, bf16[1,128,1152]{2,1,0:T(8,128)(2,1)}, u32[]{:S(2)}) copy-start(bf16[1,128,1152]{2,1,0:T(8,128)(2,1)} %param.25) | copy-start | bytes 884740
  16.9 97.5 %all-to-all-start = ((bf16[16,4,576]{2,1,0:T(4,128)(2,1)}), bf16[16,4,576]{2,1,0:T(4,128)(2,1)S(1)}, u32[]{:S(2)}, u32[]{:S(2)}) async-start(bf16[16,4,576]{2,1,0:T(4,128)(2,1)} %reshape.143), calls=%async_computation | async-start | bytes 163840 | tf_op jit(solution)/shard_map/all_to_all | solution.py:102
  28.5 136.4 %all-gather.10.cloned.1.call-start = ((), (), s32[]{:S(2)}) async-start(), calls=%async_computation.5 | async-start | bytes 2654208 | tf_op jit(solution)/shard_map/all_gather | solution.py:125
  124.6 70.8 %all-gather.8.cloned.1.call-start = ((), (), s32[]{:S(2)}) async-start(), calls=%async_computation.4 | async-start | bytes 2654208 | tf_op jit(solution)/shard_map/all_gather | solution.py:126
  125.4 136.4 %all-gather.12.cloned.1.call-start = ((), (), s32[]{:S(2)}) async-start(), calls=%async_computation.6 | async-start | bytes 2820096 | tf_op jit(solution)/shard_map/all_gather | solution.py:117
  125.9 167.4 %all-gather.14.cloned.1.call-start = ((), (), s32[]{:S(2)}) async-start(), calls=%async_computation.7 | async-start | bytes 2654208 | tf_op jit(solution)/shard_map/all_gather | solution.py:140
  169.2 30.6 %copy-start.2 = (pred[128,1024]{1,0:T(8,128)(4,1)S(1)}, pred[128,1024]{1,0:T(8,128)(4,1)}, u32[]{:S(2)}) copy-start(pred[128,1024]{1,0:T(8,128)(4,1)} %broadcast_compare_fusion) | copy-start | bytes 393220
  264.8 2.5 copy-start.6
  267.2 71.7 %reduce-scatter.2.cloned.1.call-start = ((), (), s32[]{:S(2)}) async-start(), calls=%async_computation.8 | async-start | bytes 2654208 | tf_op jit(solution)/shard_map/reduce_scatter | solution.py:146
  301.2 0.7 copy-start.4
  301.2 0.7 copy-start.13
  301.2 39.2 %copy-start.3 = (bf16[1152,16]{0,1:T(8,128)(2,1)S(1)}, bf16[1152,16]{0,1:T(8,128)(2,1)}, u32[]{:S(2)}) copy-start(bf16[1152,16]{0,1:T(8,128)(2,1)} %param.48) | copy-start | bytes 110596
  301.9 43.9 %copy-start.7 = (f32[1,4]{1,0:T(1,128)S(1)}, f32[1,4]{1,0:T(1,128)}, u32[]{:S(2)}) copy-start(f32[1,4]{1,0:T(1,128)} %param.31) | copy-start | bytes 52
  301.9 44.0 %copy-start.8 = (f32[1,4]{1,0:T(1,128)S(1)}, f32[1,4]{1,0:T(1,128)}, u32[]{:S(2)}) copy-start(f32[1,4]{1,0:T(1,128)} %param.30) | copy-start | bytes 52
  301.9 44.0 %copy-start.9 = (f32[1,4]{1,0:T(1,128)S(1)}, f32[1,4]{1,0:T(1,128)}, u32[]{:S(2)}) copy-start(f32[1,4]{1,0:T(1,128)} %param.32) | copy-start | bytes 52
  301.9 47.7 %copy-start.5 = (f32[128,8]{0,1:T(8,128)S(1)}, f32[128,8]{0,1:T(8,128)}, u32[]{:S(2)}) copy-start(f32[128,8]{0,1:T(8,128)} %param.26) | copy-start | bytes 12292
  342.6 7.0 %all-to-all-start.1 = ((f32[1,128,16]{1,0,2:T(1,128)}), f32[1,128,16]{1,0,2:T(1,128)S(1)}, u32[]{:S(2)}, u32[]{:S(2)}) async-start(f32[1,128,16]{1,0,2:T(1,128)} %bitcast.16), calls=%async_computation.2 | async-start | bytes 16384 | tf_op jit(solution)/shard_map/all_to_all | solution.py:161
Sparse Core Ops, SparseCore 0:
  9.8 107.0 all-gather.5
  124.8 40.0 all-gather.9
  166.7 28.6 all-gather.7
  197.8 63.9 all-gather.11
  267.3 26.0 all-gather.13
  301.3 37.4 reduce-scatter.1
where the time goes:
time: 358 us; the launch traced here: 357 us
  waiting for transfers between devices  182 us (51%)
  blocking collectives  82.8 us (23%)
  matrix products  39.5 us (11%)
  starting transfers between devices  15.2 us (4%)
  between operations  15 us (4%)
  local copies, waits for them, and re-layouts  12.7 us (4%)
  other arithmetic  9.78 us (3%)
    unnamed x1, blocking collectives  82.8 us
    all_gather x1, waiting for transfers between devices, shards(): lax.all_gather(out_weight, 'req', axis=1, tiled=True)  49.4 us
    all_gather x1, waiting for transfers between devices, shards(): lax.all_gather(qkv[:, width:2 * width], 'mlp', axis=0, tiled=True)  37.7 us
    reduce_scatter x1, waiting for transfers between devices, shards(): lax.psum_scatter(jnp.dot(inner, down_weight, preferred_element_type=jnp.f...  36.9 us
    all_gather x1, waiting for transfers between devices, shards(): lax.all_gather(qkv[:, 2 * width:], 'mlp', axis=0, tiled=True)  26.3 us
    all_gather x1, waiting for transfers between devices, shards(): gathered = lax.all_gather(normed_mlp, 'mlp', axis=0, tiled=True)  26.1 us
    all_to_all x1, starting transfers between devices, shards(): lax.all_to_all(local_mod, 'req', split_axis=0, concat_axis=2, tiled=True)[0]  11.6 us
    dot_general x1, matrix products, shards(): jnp.dot(inner, down_weight, preferred_element_type=jnp.float32)  7.81 us
  transfers between devices with their start and end apart: 8, of which 6 were waited for; matrix products, arithmetic and copies ran while one was open for 10% of the time, Pallas kernels for 0%

commit v1 on v0

--- a/solution.py
+++ b/solution.py
@@ -3,11 +3,33 @@
 import jax.numpy as jnp
 from jax import lax
 from jax.sharding import PartitionSpec as P
+from jax.lax import axis_index, ppermute, psum
 
 HEADS = 16
 HEAD_DIM = 72
 CLASSES = 1000
 FREQ = 256
+
+
+def keep_up_waves(arr_in):
+    block_next = psum(1, axis_name="mlp")
+    piece_now = axis_index("mlp")
+    top, last, state_now = (block_next, piece_now, arr_in.shape[0])
+    history = tuple(((b, (b + 1) % top) for b in range(top)))
+    val2 = jnp.zeros((*arr_in.shape[:0], top * state_now, *arr_in.shape[1:]), arr_in.dtype)
+    val2 = lax.dynamic_update_slice_in_dim(val2, arr_in, last * state_now, axis=0)
+    right_arr = r2 = arr_in
+    sides = tuple(((b, (b - 1) % top) for b in range(top)))
+    local_next = top // 2
+    for s in range(1, local_next + 1):
+        right_arr = ppermute(right_arr, "mlp", perm=history)
+        val2 = lax.dynamic_update_slice_in_dim(
+            val2, right_arr, (last - s) % top * state_now, axis=0
+        )
+        if s < top - local_next:
+            r2 = ppermute(r2, axis_name="mlp", perm=sides)
+            val2 = lax.dynamic_update_slice_in_dim(val2, r2, (last + s) % top * state_now, axis=0)
+    return val2
 
 
 def layer_norm(values):
@@ -123,7 +145,7 @@
     ).astype(jnp.bfloat16)
     keys_all, values_all = (
         lax.all_gather(qkv[:, width : 2 * width], "mlp", axis=0, tiled=True),
-        lax.all_gather(qkv[:, 2 * width :], "mlp", axis=0, tiled=True),
+        keep_up_waves(qkv[:, 2 * width :]),
     )
     attended = attention(
         qkv[:, :width].reshape(tok_rows, HEADS, HEAD_DIM),

time: 358 us -> 329 us (0.919)
  waiting for transfers between devices: 182 us -> 132 us
  local copies, waits for them, and re-layouts: 12.7 us -> 25 us
  starting transfers between devices: 15.2 us -> 24.2 us
    all_gather x1, waiting for transfers between devices: 37.7 us -> 0.01 us  [shards(): lax.all_gather(qkv[:, width:2 * width], 'mlp', axis=0, tiled=True)]
    all_gather x1 -> x0, waiting for transfers between devices: 26.3 us -> none  [shards(): lax.all_gather(qkv[:, 2 * width:], 'mlp', axis=0, tiled=True)]
    ppermute x0 -> x7, waiting for transfers between devices: none -> 15.1 us  [the longest x4 12.8 us: keep_up_waves(): right_arr = ppermute(right_arr, 'mlp', perm=history)]
    ppermute x0 -> x7, starting transfers between devices: none -> 8.89 us  [the longest x3 8.83 us: keep_up_waves(): r2 = ppermute(r2, axis_name='mlp', perm=sides)]
    ppermute x0 -> x7, local copies, waits for them, and re-layouts: none -> 7.2 us  [the longest x4 4.66 us: keep_up_waves(): right_arr = ppermute(right_arr, 'mlp', perm=history)]
    dynamic_update_slice x0 -> x8, local copies, waits for them, and re-layouts: none -> 6.15 us  [the longest x4 3.12 us: keep_up_waves(): lax.dynamic_update_slice_in_dim(val2, right_arr, (last - s) % top * state...]
    all_gather x1 -> x0, local copies, waits for them, and re-layouts: 4.29 us -> none  [shards(): lax.all_gather(qkv[:, 2 * width:], 'mlp', axis=0, tiled=True)]
  transfers between devices with their start and end apart: 8 -> 14, of which waited for: 6 -> 8; matrix products, arithmetic and copies ran while one was open for 10% -> 15% of each run, Pallas kernels for 0% -> 0%
where the time goes in v1:
time: 329 us; the launch traced here: 328 us
  waiting for transfers between devices  132 us (40%)
  blocking collectives  82.8 us (25%)
  matrix products  39.6 us (12%)
  local copies, waits for them, and re-layouts  25 us (8%)
  starting transfers between devices  24.2 us (7%)
  between operations  14.7 us (4%)
  other arithmetic  9.78 us (3%)
    unnamed x1, blocking collectives  82.8 us
    all_gather x1, waiting for transfers between devices, shards(): lax.all_gather(out_weight, 'req', axis=1, tiled=True)  48.5 us
    reduce_scatter x1, waiting for transfers between devices, shards(): lax.psum_scatter(jnp.dot(inner, down_weight, preferred_element_type=jnp.f...  37 us
    all_gather x1, waiting for transfers between devices, shards(): gathered = lax.all_gather(normed_mlp, 'mlp', axis=0, tiled=True)  25.9 us
    ppermute x4, waiting for transfers between devices, keep_up_waves(): right_arr = ppermute(right_arr, 'mlp', perm=history)  12.8 us
    all_to_all x1, starting transfers between devices, shards(): lax.all_to_all(local_mod, 'req', split_axis=0, concat_axis=2, tiled=True)[0]  11.6 us
    ppermute x3, starting transfers between devices, keep_up_waves(): r2 = ppermute(r2, axis_name='mlp', perm=sides)  8.83 us
    dot_general x1, matrix products, shards(): jnp.dot(inner, down_weight, preferred_element_type=jnp.float32)  7.84 us
  transfers between devices with their start and end apart: 14, of which 8 were waited for; matrix products, arithmetic and copies ran while one was open for 15% of the time, Pallas kernels for 0%

profile of v1, /device:TPU:8, one launch (start us, length us, event | category | flops | bytes accessed | tf_op | source)
XLA Modules:
  0.0 327.7 jit_solution(4099172147767852730)
XLA Ops:
  13.2 3.0 fusion.29
  16.9 11.6 %all-to-all-start = ((bf16[16,4,576]{2,1,0:T(4,128)(2,1)}), bf16[16,4,576]{2,1,0:T(4,128)(2,1)S(1)}, u32[]{:S(2)}, u32[]{:S(2)}) async-start(bf16[16,4,576]{2,1,0:T(4,128)(2,1)} %reshape.143), calls=%async_computation | async-start | bytes 163840 | tf_op jit(solution)/shard_map/all_to_all | solution.py:124
  31.1 82.8 %all-reduce.2 = (bf16[3456]{0:T(1024)(128)(2,1)S(1)}, bf16[1152]{0:T(1024)(128)(2,1)S(1)}) all-reduce(bf16[3456]{0:T(1024)(128)(2,1)S(1)} %dynamic-update-slice, bf16[1152]{0:T(1024)(128)(2,1)S(1)} %dynamic-update-slice.1), channel_id=1, replica_groups=mesh['cfg'=2,'req'=16,'mlp'=8] {'req'}, use_global_device_ids=true, to_apply=%add | all-reduce | flops 4608 | bytes 18432
  114.6 3.0 fusion.67
  117.6 6.1 %fusion.2 = bf16[128,3456]{1,0:T(8,128)(2,1)S(1)} fusion(bf16[1152,3456]{0,1:T(8,128)(2,1)} %all-gather.5.cloned.1.call-done, f32[3456]{0:T(1024)S(1)} %convert_element_type.103, bf16[1,128,1152]{2,1,0:T(8,128)(2,1)S(1)} %copy-done.1, f32[128,9216]{1,0:T(8,128)} %fusion.67, f32[128]{0:T(128)S(1)} %add_rsqrt_fusion.2, f32[128]{0:T(128)S(1)} %broadcast_multiply_fusion.2), kind=kOutput, calls=%fused_computation.5 | convolution fusion | flops 1021132800 | bytes 10336768 | tf_op jit(solution)/shard_map/dot_general | solution.py:143
  127.2 2.9 collective-permute-start.1
  136.6 3.0 collective-permute-start.3
  140.4 1.9 collective-permute-done.2
  144.6 2.9 collective-permute-start.5
  148.2 3.0 collective-permute-done.4
  153.1 2.3 collective-permute-done.5
  157.4 7.8 %collective-permute-done.6 = bf16[128,1152]{1,0:T(8,128)(2,1)} collective-permute-done((bf16[128,1152]{1,0:T(8,128)(2,1)}, bf16[128,1152]{1,0:T(8,128)(2,1)}, u32[]{:S(2)}, u32[]{:S(2)}) %collective-permute-start.6) | collective-permute-done | bytes 294944 | tf_op jit(solution)/shard_map/ppermute | solution.py:25
  167.2 4.3 %copy.80 = bf16[1024,1152]{0,1:T(8,128)(2,1)} copy(bf16[1024,1152]{1,0:T(8,128)(2,1)} %all-gather.7.cloned.1.call-done) | data formatting | bytes 4718592 | tf_op jit(solution)/shard_map/all_gather | solution.py:147
  171.5 7.5 %fusion.84 = (f32[16,128]{1,0:T(8,128)S(1)}, bf16[16,128,1024]{2,1,0:T(8,128)(2,1)}) fusion(pred[128,1024]{1,0:T(8,128)(4,1)S(1)} %copy-done.4, bf16[128,16,72]{0,2,1:T(8,128)(2,1)S(1)} %bitcast.87, bf16[1024,16,72]{0,2,1:T(8,128)(2,1)} %bitcast.84), kind=kOutput, calls=%fused_computation.120 | convolution fusion | flops 314573824 | bytes 6987776 | tf_op jit(solution)/shard_map/sub | solution.py:61
  179.0 5.3 %fusion.26 = bf16[128,16,72]{0,2,1:T(8,128)(2,1)} fusion(bf16[1024,16,72]{0,2,1:T(8,128)(2,1)} %bitcast.8, bf16[16,128,1024]{2,1,0:T(8,128)(2,1)} %get-tuple-element.18, f32[128,16]{0,1:T(8,128)S(1)} %bitcast.94), kind=kOutput, calls=%fused_computation.31 | convolution fusion | flops 302284800 | bytes 6856704 | tf_op jit(solution)/shard_map/hqk,khd->qhd/dot_general | solution.py:64
  184.2 48.5 %all-gather.9.cloned.1.call-done = bf16[1152,1152]{0,1:T(8,128)(2,1)} async-done(((bf16[1152,72]{0,1:T(8,128)(2,1)}), bf16[1152,1152]{0,1:T(8,128)(2,1)}) %all-gather.9.cloned.1.call-update) | async-done | bytes 2654224 | tf_op jit(solution)/shard_map/all_gather | solution.py:139
  232.7 3.0 fusion.85
  235.9 2.2 fusion.41
  238.4 25.9 %all-gather.11.cloned.1.call-done = bf16[1024,1152]{1,0:T(8,128)(2,1)} async-done(((bf16[128,1152]{1,0:T(8,128)(2,1)}), bf16[1024,1152]{1,0:T(8,128)(2,1)}) %all-gather.11.cloned.1.call-update) | async-done | bytes 2359312 | tf_op jit(solution)/shard_map/all_gather | solution.py:162
  264.3 7.8 %convolution_convert_fusion = bf16[1024,1152]{1,0:T(8,128)(2,1)} fusion(bf16[576,1152]{1,0:T(8,128)(2,1)} %param.46, bf16[1024,1152]{1,0:T(8,128)(2,1)} %all-gather.11.cloned.1.call-done, bf16[1152,576]{0,1:T(8,128)(2,1)} %param.44, f32[576]{0:T(1024)S(1)} %convert_element_type.111), kind=kOutput, calls=%fused_computation.11 | convolution fusion | flops 2724986880 | bytes 7375104 | tf_op jit(solution)/shard_map/dot_general | solution.py:169
  272.8 37.0 %reduce-scatter.2.cloned.1.call-done = bf16[128,1152]{1,0:T(8,128)(2,1)} async-done(((bf16[1024,1152]{1,0:T(8,128)(2,1)}), bf16[128,1152]{1,0:T(8,128)(2,1)}) %reduce-scatter.2.cloned.1.call-update) | async-done | bytes 294928 | tf_op jit(solution)/shard_map/reduce_scatter | solution.py:168
  311.4 2.2 convolution_add_fusion.6
  313.6 3.2 all-to-all-start.1
  316.9 3.7 %all-to-all-done.1 = f32[1,128,16]{1,0,2:T(1,128)S(1)} async-done(((f32[1,128,16]{1,0,2:T(1,128)}), f32[1,128,16]{1,0,2:T(1,128)S(1)}, u32[]{:S(2)}, u32[]{:S(2)}) %all-to-all-start.1) | async-done | bytes 8224 | tf_op jit(solution)/shard_map/all_to_all | solution.py:183
  (115 shorter events, 32.2 us)
Async XLA Ops:
  6.5 111.0 %all-gather.5.cloned.1.call-start = ((), (), s32[]{:S(2)}) async-start(), calls=%async_computation.3 | async-start | bytes 8460288 | tf_op jit(solution)/shard_map/all_gather | solution.py:137
  13.2 15.4 %copy-start.12 = (s32[1,4]{1,0:T(1,128)S(1)}, s32[1,4]{1,0:T(1,128)}, u32[]{:S(2)}) copy-start(s32[1,4]{1,0:T(1,128)} %param.29) | copy-start | bytes 52
  13.2 15.5 %copy-start.16 = (u32[256]{0:T(256)S(1)}, u32[256]{0:T(256)}, u32[]{:S(2)}) copy-start(u32[256]{0:T(256)} %constant.123) | copy-start | bytes 3076
  13.2 17.4 %copy-start.13 = (bf16[216]{0:T(256)(128)(2,1)S(1)}, bf16[216]{0:T(256)(128)(2,1)}, u32[]{:S(2)}) copy-start(bf16[216]{0:T(256)(128)(2,1)} %param.41) | copy-start | bytes 1300
  13.2 17.7 %copy-start.14 = (bf16[72]{0:T(256)(128)(2,1)S(1)}, bf16[72]{0:T(256)(128)(2,1)}, u32[]{:S(2)}) copy-start(bf16[72]{0:T(256)(128)(2,1)} %param.43) | copy-start | bytes 436
  13.2 100.9 %copy-start.1 = (bf16[1,128,1152]{2,1,0:T(8,128)(2,1)S(1)}, bf16[1,128,1152]{2,1,0:T(8,128)(2,1)}, u32[]{:S(2)}) copy-start(bf16[1,128,1152]{2,1,0:T(8,128)(2,1)} %param.25) | copy-start | bytes 884740
  16.9 97.5 %all-to-all-start = ((bf16[16,4,576]{2,1,0:T(4,128)(2,1)}), bf16[16,4,576]{2,1,0:T(4,128)(2,1)S(1)}, u32[]{:S(2)}, u32[]{:S(2)}) async-start(bf16[16,4,576]{2,1,0:T(4,128)(2,1)} %reshape.143), calls=%async_computation | async-start | bytes 163840 | tf_op jit(solution)/shard_map/all_to_all | solution.py:124
  28.5 138.7 %all-gather.7.cloned.1.call-start = ((), (), s32[]{:S(2)}) async-start(), calls=%async_computation.4 | async-start | bytes 2654208 | tf_op jit(solution)/shard_map/all_gather | solution.py:147
  124.5 108.1 %all-gather.9.cloned.1.call-start = ((), (), s32[]{:S(2)}) async-start(), calls=%async_computation.5 | async-start | bytes 2820096 | tf_op jit(solution)/shard_map/all_gather | solution.py:139
  125.3 139.0 %all-gather.11.cloned.1.call-start = ((), (), s32[]{:S(2)}) async-start(), calls=%async_computation.6 | async-start | bytes 2654208 | tf_op jit(solution)/shard_map/all_gather | solution.py:162
  125.5 8.0 %collective-permute-start = (bf16[128,1152]{1,0:T(8,128)(2,1)S(1)}, bf16[128,1152]{1,0:T(8,128)(2,1)}, u32[]{:S(2)}, u32[]{:S(2)}) collective-permute-start(bf16[128,1152]{1,0:T(8,128)(2,1)S(1)} %get-tuple-element.14), channel_id=1, source_target_pairs={{0,1},{1,2},{2,3},{3,4},{4,5},{5,6},{6,7},{7,0},{8,9},{9,10},{10,1... | collective-permute-start | bytes 884744 | tf_op jit(solution)/shard_map/ppermute | solution.py:25
  127.2 8.2 %collective-permute-start.1 = (bf16[128,1152]{1,0:T(8,128)(2,1)S(1)}, bf16[128,1152]{1,0:T(8,128)(2,1)}, u32[]{:S(2)}, u32[]{:S(2)}) collective-permute-start(bf16[128,1152]{1,0:T(8,128)(2,1)S(1)} %get-tuple-element.14), channel_id=1, source_target_pairs={{0,7},{1,0},{2,1},{3,2},{4,3},{5,4},{6,5},{7,6},{8,15},{9,8},{10,9... | collective-permute-start | bytes 884744 | tf_op jit(solution)/shard_map/ppermute | solution.py:30
  134.7 7.7 %collective-permute-start.2 = (bf16[128,1152]{1,0:T(8,128)(2,1)}, bf16[128,1152]{1,0:T(8,128)(2,1)}, u32[]{:S(2)}, u32[]{:S(2)}) collective-permute-start(bf16[128,1152]{1,0:T(8,128)(2,1)} %collective-permute-done), channel_id=1, source_target_pairs={{0,1},{1,2},{2,3},{3,4},{4,5},{5,6},{6,7},{7,0},{8,9},{9,10},{10,1... | collective-permute-start | bytes 884744 | tf_op jit(solution)/shard_map/ppermute | solution.py:25
  136.6 7.7 %collective-permute-start.3 = (bf16[128,1152]{1,0:T(8,128)(2,1)}, bf16[128,1152]{1,0:T(8,128)(2,1)S(1)}, u32[]{:S(2)}, u32[]{:S(2)}) collective-permute-start(bf16[128,1152]{1,0:T(8,128)(2,1)} %collective-permute-done.1), channel_id=1, source_target_pairs={{0,7},{1,0},{2,1},{3,2},{4,3},{5,4},{6,5},{7,6},{8,15},{9,8},{10,9... | collective-permute-start | bytes 884744 | tf_op jit(solution)/shard_map/ppermute | solution.py:30
  143.5 7.7 %collective-permute-start.4 = (bf16[128,1152]{1,0:T(8,128)(2,1)}, bf16[128,1152]{1,0:T(8,128)(2,1)}, u32[]{:S(2)}, u32[]{:S(2)}) collective-permute-start(bf16[128,1152]{1,0:T(8,128)(2,1)} %collective-permute-done.2), channel_id=1, source_target_pairs={{0,1},{1,2},{2,3},{3,4},{4,5},{5,6},{6,7},{7,0},{8,9},{9,10},{10,1... | collective-permute-start | bytes 884744 | tf_op jit(solution)/shard_map/ppermute | solution.py:25
  144.6 10.9 %collective-permute-start.5 = (bf16[128,1152]{1,0:T(8,128)(2,1)S(1)}, bf16[128,1152]{1,0:T(8,128)(2,1)}, u32[]{:S(2)}, u32[]{:S(2)}) collective-permute-start(bf16[128,1152]{1,0:T(8,128)(2,1)S(1)} %collective-permute-done.3), channel_id=1, source_target_pairs={{0,7},{1,0},{2,1},{3,2},{4,3},{5,4},{6,5},{7,6},{8,15},{9,8},{10,9... | collective-permute-start | bytes 884744 | tf_op jit(solution)/shard_map/ppermute | solution.py:30
  152.4 12.9 %collective-permute-start.6 = (bf16[128,1152]{1,0:T(8,128)(2,1)}, bf16[128,1152]{1,0:T(8,128)(2,1)}, u32[]{:S(2)}, u32[]{:S(2)}) collective-permute-start(bf16[128,1152]{1,0:T(8,128)(2,1)} %collective-permute-done.4), channel_id=1, source_target_pairs={{0,1},{1,2},{2,3},{3,4},{4,5},{5,6},{6,7},{7,0},{8,9},{9,10},{10,1... | collective-permute-start | bytes 884744 | tf_op jit(solution)/shard_map/ppermute | solution.py:25
  238.1 71.7 %reduce-scatter.2.cloned.1.call-start = ((), (), s32[]{:S(2)}) async-start(), calls=%async_computation.7 | async-start | bytes 2654208 | tf_op jit(solution)/shard_map/reduce_scatter | solution.py:168
  272.1 39.3 %copy-start.5 = (bf16[1152,16]{0,1:T(8,128)(2,1)S(1)}, bf16[1152,16]{0,1:T(8,128)(2,1)}, u32[]{:S(2)}) copy-start(bf16[1152,16]{0,1:T(8,128)(2,1)} %param.48) | copy-start | bytes 110596
  272.8 44.0 %copy-start.9 = (f32[1,4]{1,0:T(1,128)S(1)}, f32[1,4]{1,0:T(1,128)}, u32[]{:S(2)}) copy-start(f32[1,4]{1,0:T(1,128)} %param.31) | copy-start | bytes 52
  272.8 44.0 %copy-start.10 = (f32[1,4]{1,0:T(1,128)S(1)}, f32[1,4]{1,0:T(1,128)}, u32[]{:S(2)}) copy-start(f32[1,4]{1,0:T(1,128)} %param.30) | copy-start | bytes 52
  272.8 44.0 %copy-start.11 = (f32[1,4]{1,0:T(1,128)S(1)}, f32[1,4]{1,0:T(1,128)}, u32[]{:S(2)}) copy-start(f32[1,4]{1,0:T(1,128)} %param.32) | copy-start | bytes 52
  272.8 47.8 %copy-start.7 = (f32[128,8]{0,1:T(8,128)S(1)}, f32[128,8]{0,1:T(8,128)}, u32[]{:S(2)}) copy-start(f32[128,8]{0,1:T(8,128)} %param.26) | copy-start | bytes 12292
  313.6 7.0 %all-to-all-start.1 = ((f32[1,128,16]{1,0,2:T(1,128)}), f32[1,128,16]{1,0,2:T(1,128)S(1)}, u32[]{:S(2)}, u32[]{:S(2)}) async-start(f32[1,128,16]{1,0,2:T(1,128)} %bitcast.16), calls=%async_computation.2 | async-start | bytes 16384 | tf_op jit(solution)/shard_map/all_to_all | solution.py:183
  (7 other events, 22.2 us)
Sparse Core Ops, SparseCore 0:
  9.8 105.5 all-gather.4
  124.7 42.0 all-gather.6
  169.3 63.3 all-gather.8
  238.2 26.0 all-gather.10
  272.3 37.5 reduce-scatter.1
